TPU v7x, 256 devices: a whole 4x4x8 slice. The times are simulated.
256 devices in a mesh: req: 128 (over z, y, x), tensor: 2 (over core).
Axes of the slice: x: 4, y: 4, z: 8, core: 2. Of those that a mesh axis runs over, the one named last changes fastest.
Arguments:
- patches: bfloat16 [256, 256, 1280], P('req'), may hold values from -6 to 6
- grids: int32 [256, 2], replicated, may hold values from 2 to 16, as said below
- place: int32 [256], replicated, may hold values from 0 to 255, as said below
- text_tokens: bfloat16 [128, 384, 1280], P('req'), may hold values from -6 to 6
- encoder_attend_in: bfloat16 [1280, 3, 1280], P(None, None, 'tensor'), may hold values from -0.15625 to 0.15625
- encoder_attend_out: bfloat16 [1280, 1280], P('tensor'), may hold values from -0.15625 to 0.15625
- encoder_expand: bfloat16 [1280, 5120], P(None, 'tensor'), may hold values from -0.15625 to 0.15625
- encoder_contract: bfloat16 [5120, 1280], P('tensor'), may hold values from -0.078125 to 0.078125
- encoder_gain_first: float32 [1280], replicated, may hold values from 0.25 to 1.75
- encoder_gain_second: float32 [1280], replicated, may hold values from 0.25 to 1.75
- merge_weight: bfloat16 [5120, 1280], P(None, 'tensor'), may hold values from -0.078125 to 0.078125
- decoder_attend_in: bfloat16 [1280, 3, 1280], P(None, None, 'tensor'), may hold values from -0.15625 to 0.15625
- decoder_attend_out: bfloat16 [1280, 1280], P('tensor'), may hold values from -0.15625 to 0.15625
- decoder_expand: bfloat16 [1280, 5120], P(None, 'tensor'), may hold values from -0.15625 to 0.15625
- decoder_contract: bfloat16 [5120, 1280], P('tensor'), may hold values from -0.078125 to 0.078125
- decoder_gain_first: float32 [1280], replicated, may hold values from 0.25 to 1.75
- decoder_gain_second: float32 [1280], replicated, may hold values from 0.25 to 1.75
Outputs:
- decoded: bfloat16 [128, 512, 1280], P('req')
Inputs may be any that keep to these rules, and one draw needn't show every extreme that they name: `grids`: both entries are even; image 0 always has the full 16 x 16 grid. A permutation: image i's merged tokens go to request place[i] // 2, image slot place[i] % 2. The request index, taken bitwise exclusive-or with i // 2, depends on i % 2 only: it is 1 when i % 2 = 0 and 64 when i % 2 = 1.
All inputs are finite; a program needn't handle non-finite values.
Results may differ from a plain program's by a relative error of at most 0.015.
Values may be sent and summed in bfloat16 or wider, within the bound.
No kernel may reach another device: no remote copies, remote signals or barrier semaphores. Data moves between devices by JAX's collectives and lax.ppermute only.
A program may use at most 192 MiB of HBM per device.

v0:
```python
import jax
import jax.numpy as jnp
from jax import lax
from jax.sharding import PartitionSpec as P

HEAD_DIM = 80
GRID = 16


def normalize(values, gain):
    center = values - jnp.mean(values, axis=-1, keepdims=True)
    spread = jnp.mean(center * center, axis=-1, keepdims=True)
    return center * lax.rsqrt(spread + 1e-06) * gain


def attend(normed, allowed, attend_in, attend_out):
    batch, length, width = normed.shape
    projected = jnp.dot(
        normed, attend_in.reshape(width, -1), preferred_element_type=jnp.float32
    ).astype(jnp.bfloat16)
    projected = projected.reshape(batch, length, 3, -1, HEAD_DIM)
    queries = projected[:, :, 0]
    key_rows = projected[:, :, 1]
    value_rows = projected[:, :, 2]
    scores = jnp.einsum(
        "bqhd,bkhd->bhqk", queries, key_rows, preferred_element_type=jnp.float32
    ) * HEAD_DIM ** (-0.5)
    scores = jnp.where(allowed[:, None], scores, jnp.float32(-1e30))
    probs = jax.nn.softmax(scores, axis=-1).astype(jnp.bfloat16)
    mixed = jnp.einsum(
        "bhqk,bkhd->bqhd", probs, value_rows, preferred_element_type=jnp.float32
    ).astype(jnp.bfloat16)
    return jnp.dot(mixed.reshape(batch, length, -1), attend_out, preferred_element_type=jnp.float32)


def layer(inputs, allowed, attend_in, attend_out, expand, contract, gain_first, gain_second):
    widened = inputs.astype(jnp.float32)
    first = normalize(widened, gain_first).astype(jnp.bfloat16)
    attended = attend(first, allowed, attend_in, attend_out)
    residual = widened + lax.psum(attended.astype(jnp.bfloat16), "tensor").astype(jnp.float32)
    second = normalize(residual, gain_second).astype(jnp.bfloat16)
    hidden = jax.nn.gelu(
        jnp.dot(second, expand, preferred_element_type=jnp.float32), approximate=False
    ).astype(jnp.bfloat16)
    partial_out = jnp.dot(hidden, contract, preferred_element_type=jnp.float32)
    return (
        residual + lax.psum(partial_out.astype(jnp.bfloat16), "tensor").astype(jnp.float32)
    ).astype(jnp.bfloat16)


def on_device(
    patches,
    grids,
    place,
    text_tokens,
    encoder_attend_in,
    encoder_attend_out,
    encoder_expand,
    encoder_contract,
    encoder_gain_first,
    encoder_gain_second,
    merge_weight,
    decoder_attend_in,
    decoder_attend_out,
    decoder_expand,
    decoder_contract,
    decoder_gain_first,
    decoder_gain_second,
):
    device = lax.axis_index("req")
    images_here, cell_count, width = patches.shape
    side = GRID
    half = side // 2
    slot_count = half * half
    local_grids = lax.dynamic_slice_in_dim(grids, device * images_here, images_here, 0)
    cells = jnp.arange(cell_count)
    cell_valid = ((cells // side)[None, :] < local_grids[:, 0:1]) & (
        (cells % side)[None, :] < local_grids[:, 1:2]
    )
    image_allowed = jnp.broadcast_to(cell_valid[:, None, :], (images_here, cell_count, cell_count))
    encoded = layer(
        patches,
        image_allowed,
        encoder_attend_in,
        encoder_attend_out,
        encoder_expand,
        encoder_contract,
        encoder_gain_first,
        encoder_gain_second,
    )
    blocks = (
        encoded.reshape(images_here, half, 2, half, 2, width)
        .transpose(0, 1, 3, 2, 4, 5)
        .reshape(images_here * slot_count, 4 * width)
    )
    merged = jnp.dot(blocks, merge_weight, preferred_element_type=jnp.float32).astype(jnp.bfloat16)
    merged = merged.reshape(images_here, slot_count, -1)
    wanted = device * images_here + jnp.arange(images_here)
    matches = place[None, :] == wanted[:, None]
    everything = lax.all_gather(merged, "req", axis=0, tiled=True)
    arranged = jnp.einsum(
        "qg,gmc->qmc", matches.astype(jnp.bfloat16), everything, preferred_element_type=jnp.float32
    ).astype(jnp.bfloat16)
    slot_grids = jnp.sum(matches.astype(jnp.int32)[:, :, None] * grids[None, :, :], axis=1)
    slots = jnp.arange(slot_count)
    merged_valid = ((2 * (slots // half))[None, :] < slot_grids[:, 0:1]) & (
        (2 * (slots % half))[None, :] < slot_grids[:, 1:2]
    )
    image_rows = lax.all_gather(
        arranged.reshape(images_here * slot_count, -1), "tensor", axis=1, tiled=True
    )
    prompt = jnp.concatenate([image_rows, text_tokens[0]], axis=0)[None]
    text_count = text_tokens.shape[1]
    prompt_valid = jnp.concatenate(
        [merged_valid.reshape(-1), jnp.ones((text_count,), bool)], axis=0
    )
    length = prompt.shape[1]
    positions = jnp.arange(length)
    prompt_allowed = (prompt_valid[None, :] & (positions[None, :] <= positions[:, None]))[None]
    decoded = layer(
        prompt,
        prompt_allowed,
        decoder_attend_in,
        decoder_attend_out,
        decoder_expand,
        decoder_contract,
        decoder_gain_first,
        decoder_gain_second,
    )
    return jnp.where(prompt_valid[None, :, None], decoded, jnp.zeros_like(decoded))


def solution(mesh):
    placed = (
        P("req", None, None),
        P(),
        P(),
        P("req", None, None),
        P(None, None, "tensor"),
        P("tensor", None),
        P(None, "tensor"),
        P("tensor", None),
        P(),
        P(),
        P(None, "tensor"),
        P(None, None, "tensor"),
        P("tensor", None),
        P(None, "tensor"),
        P("tensor", None),
        P(),
        P(),
    )
    return jax.shard_map(
        on_device, mesh=mesh, in_specs=placed, out_specs=P("req", None, None), check_vma=False
    )
```

profile of v0, /device:TPU:1, one launch (start us, length us, event | category | flops | bytes accessed | tf_op | source)
XLA Modules:
  0.0 464.2 jit_solution(3344915803614442546)
XLA Ops:
  6.5 0.9 constant_dynamic-slice_fusion
  7.4 1.6 convert_reduce_fusion.1
  9.0 1.8 fusion.41
  10.8 8.3 %copy.73 = bf16[1280,3,640]{0,2,1:T(8,128)(2,1)} copy(bf16[1280,3,640]{2,0,1:T(8,128)(2,1)} %param.21) | data formatting | bytes 9830400 | tf_op args[4]
  19.1 6.7 %convolution_convert_fusion.4 = bf16[2,256,1920]{2,1,0:T(8,128)(2,1)} fusion(bf16[1280,1920,1]{0,1,2:T(8,128)(2,1)} %bitcast.112, bf16[2,256,1280]{2,1,0:T(8,128)(2,1)S(1)} %copy-done.2, f32[1280]{0:T(1024)S(1)} %copy-done.9, f32[2,256]{1,0:T(2,128)S(1)} %add_rsqrt_fusion.3, f32[2,256]{1,0:T(2,128)S(1)} %broadcast_multiply_fusion.3), kind=kOutput, calls=%fused_computation.74 | convolution fusion | flops 2520842240 | bytes 8201216 | tf_op jit(solution)/shard_map/dot_general | solution.py:18
  25.8 4.0 copy.75
  29.8 2.0 fusion.153
  31.8 0.1 compare_and_fusion
  31.9 1.5 fusion.227
  33.5 1.6 fusion.114
  35.1 2.3 convolution_convert_fusion.1
  37.4 0.3 all-reduce.8.cloned.1.call-start
  37.6 35.2 %all-reduce.6.cloned.1.call-done = bf16[2,256,1280]{2,1,0:T(8,128)(2,1)} async-done(((bf16[2,256,1280]{2,1,0:T(8,128)(2,1)}), bf16[2,256,1280]{2,1,0:T(8,128)(2,1)}) %all-reduce.6.cloned.1.call-update) | async-done | bytes 1310736 | tf_op jit(solution)/shard_map/psum | solution.py:40
  72.8 1.8 fusion.107
  74.7 2.1 multiply_reduce_fusion.1
  76.8 8.1 %fusion.144 = (u8[256,2560]{1,0:T(8,128)(4,1)S(1)}, u8[256,2560]{1,0:T(8,128)(4,1)S(1)}, f32[2,256,2560]{2,1,0:T(8,128)S(1)}) fusion(bf16[1280,2560]{1,0:T(8,128)(2,1)} %param.23, bf16[2,256,1280]{2,1,0:T(8,128)(2,1)S(1)} %copy-done.4, bf16[2,256,1280]{2,1,0:T(8,128)(2,1)S(1)} %copy-done.2, f32[1280]{0:T(1024)S(1)} %copy-done.10, ...), kind=kOutput, calls=%fused_computation.179 | convolution fusion | flops 3375759360 | bytes 15737856 | tf_op jit(solution)/shard_map/dot_general | solution.py:43
  84.9 16.2 %fusion.35 = bf16[2,256,1280]{2,1,0:T(8,128)(2,1)} fusion(bf16[2560,1280]{1,0:T(8,128)(2,1)S(1)} %bitcast.118, f32[2,256,2560]{2,1,0:T(8,128)S(1)} %get-tuple-element.13, u8[256,2560]{1,0:T(8,128)(4,1)S(1)} %get-tuple-element.6, u8[256,2560]{1,0:T(8,128)(4,1)S(1)} %get-tuple-element.5), kind=kOutput, calls=%fused_computation.71 | convolution fusion | flops 3447848960 | bytes 14417920 | tf_op jit(solution)/shard_map/dot_general | solution.py:45
  101.1 0.0 all-gather.2.cloned.1.call-start
  101.2 32.2 %all-reduce.8.cloned.1.call-done = bf16[2,256,1280]{2,1,0:T(8,128)(2,1)} async-done(((bf16[2,256,1280]{2,1,0:T(8,128)(2,1)}), bf16[2,256,1280]{2,1,0:T(8,128)(2,1)}) %all-reduce.8.cloned.1.call-update) | async-done | bytes 1310736 | tf_op jit(solution)/shard_map/psum | solution.py:47
  133.4 2.8 add_convert_fusion.1
  136.2 3.1 reshape.449
  139.3 1.0 copy.100
  140.3 1.0 reshape.450
  141.3 4.7 %convolution_convert_fusion.5 = bf16[128,640]{1,0:T(8,128)(2,1)} fusion(bf16[128,5120]{1,0:T(8,128)(2,1)S(1)} %reshape.450, bf16[5120,640]{1,0:T(8,128)(2,1)} %param.27), kind=kOutput, calls=%fused_computation.181 | convolution fusion | flops 838942720 | bytes 8028160 | tf_op jit(solution)/shard_map/dot_general | solution.py:96
  146.1 8.6 %copy.84 = bf16[1280,3,640]{0,2,1:T(8,128)(2,1)} copy(bf16[1280,3,640]{2,0,1:T(8,128)(2,1)} %param.28) | data formatting | bytes 9830400 | tf_op args[11]
  154.8 0.1 compare_convert_fusion
  154.9 0.1 multiply_reduce_fusion.2
  155.0 0.2 slice_reduce_fusion.1
  155.2 0.1 compare_and_fusion.1
  155.3 0.1 and.76
  155.4 0.1 fusion.148
  155.6 155.3 %all-gather.2.cloned.1.call-done = bf16[256,64,640]{2,1,0:T(8,128)(2,1)} async-done(((bf16[2,64,640]{2,1,0:T(8,128)(2,1)}), bf16[256,64,640]{2,1,0:T(8,128)(2,1)}) %all-gather.2.cloned.1.call-update) | async-done | bytes 20971536 | tf_op jit(solution)/shard_map/all_gather | solution.py:100
  310.9 29.1 %fusion.145 = bf16[2,64,640]{2,0,1:T(2,128)(2,1)S(1)} fusion(bf16[256,64,640]{2,1,0:T(8,128)(2,1)} %all-gather.2.cloned.1.call-done, s32[256]{0:T(256)S(1)} %copy-done.7, s32[2]{0:T(128)S(1)} %iota_add_fusion), kind=kOutput, calls=%fused_computation.180 | convolution fusion | flops 42025472 | bytes 21136392 | tf_op jit(solution)/shard_map/qg,gmc->qmc/dot_general | solution.py:101
  340.0 2.7 all_gather.7
  342.7 0.2 convert_reduce_fusion
  342.9 0.5 fusion.45
  343.5 4.6 convolution_convert_fusion.3
  348.1 4.0 copy.85
  352.1 7.7 %fusion.228 = (f32[8,512]{1,0:T(8,128)S(1)}, f32[8,512,512]{1,2,0:T(8,128)}) fusion(pred[512,512]{0,1:T(8,128)(4,1)S(1)} %fusion.148, bf16[1,512,3,8,80]{1,4,3,2,0:T(8,128)(2,1)} %bitcast.113), kind=kOutput, calls=%fused_computation.297 | convolution fusion | flops 343933440 | bytes 9977856 | tf_op jit(solution)/shard_map/sub | solution.py:29
  359.7 4.6 fusion.115
  364.3 2.3 fusion.39
  366.6 0.3 all-reduce.12.cloned.1.call-start
  366.9 28.2 %all-reduce.10.cloned.1.call-done = bf16[1,512,1280]{2,1,0:T(8,128)(2,1)} async-done(((bf16[1,512,1280]{2,1,0:T(8,128)(2,1)}), bf16[1,512,1280]{2,1,0:T(8,128)(2,1)}) %all-reduce.10.cloned.1.call-update) | async-done | bytes 1310736 | tf_op jit(solution)/shard_map/psum | solution.py:40
  395.1 1.7 fusion.108
  396.8 1.9 multiply_reduce_fusion
  398.7 22.9 %fusion.38 = bf16[1,512,1280]{2,1,0:T(8,128)(2,1)} fusion(bf16[2560,1280]{1,0:T(8,128)(2,1)} %param.31, bf16[1280,2560]{1,0:T(8,128)(2,1)} %param.30, bf16[1,512,1280]{2,1,0:T(8,128)(2,1)} %all-reduce.10.cloned.1.call-done, f32[1280]{0:T(1024)S(1)} %copy-done.12, f32[512]{0:T(512)S(1)} %add_rsqrt_fusion, f32[512]{0:T(512)S(1)} %broadcast_multiply_fusion, ...), kind=kOutput, calls=%fused_computation.75 | convolution fusion | flops 6803292160 | bytes 17048576 | tf_op jit(solution)/shard_map/dot_general | solution.py:45
  421.6 32.2 %all-reduce.12.cloned.1.call-done = bf16[1,512,1280]{2,1,0:T(8,128)(2,1)} async-done(((bf16[1,512,1280]{2,1,0:T(8,128)(2,1)}), bf16[1,512,1280]{2,1,0:T(8,128)(2,1)}) %all-reduce.12.cloned.1.call-update) | async-done | bytes 1310736 | tf_op jit(solution)/shard_map/psum | solution.py:47
  453.9 3.3 fusion.123
  (52 shorter events, 0.3 us)
Async XLA Ops:
  6.5 28.5 %copy-start = (bf16[640,1280]{1,0:T(8,128)(2,1)S(1)}, bf16[640,1280]{1,0:T(8,128)(2,1)}, u32[]{:S(2)}) copy-start(bf16[640,1280]{1,0:T(8,128)(2,1)} %param.22) | copy-start | bytes 4915204
  6.5 66.3 %all-reduce.6.cloned.1.call-start = ((), (), s32[]{:S(2)}) async-start(), calls=%async_computation | async-start | bytes 2621440 | tf_op jit(solution)/shard_map/psum | solution.py:40
  10.8 8.3 %copy-start.2 = (bf16[2,256,1280]{2,1,0:T(8,128)(2,1)S(1)}, bf16[2,256,1280]{2,1,0:T(8,128)(2,1)}, u32[]{:S(2)}) copy-start(bf16[2,256,1280]{2,1,0:T(8,128)(2,1)} %param.17) | copy-start | bytes 3932164
  10.8 8.3 %copy-start.9 = (f32[1280]{0:T(1024)S(1)}, f32[1280]{0:T(1024)}, u32[]{:S(2)}) copy-start(f32[1280]{0:T(1024)} %param.25) | copy-start | bytes 15364
  35.1 41.7 %copy-start.10 = (f32[1280]{0:T(1024)S(1)}, f32[1280]{0:T(1024)}, u32[]{:S(2)}) copy-start(f32[1280]{0:T(1024)} %param.26) | copy-start | bytes 15364
  37.4 96.0 %all-reduce.8.cloned.1.call-start = ((), (), s32[]{:S(2)}) async-start(), calls=%async_computation.1 | async-start | bytes 2621440 | tf_op jit(solution)/shard_map/psum | solution.py:47
  72.8 3.9 copy-start.4
  74.7 10.2 %slice-start = ((s8[6553600]{0:T(1024)(128)(4,1)}), s8[4194304]{0:T(1024)(128)(4,1)S(1)}, s32[]{:S(2)}) async-start(s8[6553600]{0:T(1024)(128)(4,1)} %bitcast.117), calls=%async_computation.5 | async-start | bytes 8388608
  76.8 8.1 %slice-start.1 = ((s8[6553600]{0:T(1024)(128)(4,1)}), s8[2359296]{0:T(1024)(128)(4,1)S(1)}, s32[]{:S(2)}) async-start(s8[6553600]{0:T(1024)(128)(4,1)} %bitcast.117), calls=%async_computation.6 | async-start | bytes 4718592
  101.1 209.7 %all-gather.2.cloned.1.call-start = ((), (), s32[]{:S(2)}) async-start(), calls=%async_computation.2 | async-start | bytes 21135360 | tf_op jit(solution)/shard_map/all_gather | solution.py:100
  146.0 8.8 %copy-start.7 = (s32[256]{0:T(256)S(1)}, s32[256]{0:T(256)}, u32[]{:S(2)}) copy-start(s32[256]{0:T(256)} %param.19) | copy-start | bytes 3076
  146.1 8.8 %copy-start.6 = (s32[256,2]{0,1:T(2,128)S(1)}, s32[256,2]{0,1:T(2,128)}, u32[]{:S(2)}) copy-start(s32[256,2]{0,1:T(2,128)} %param.18) | copy-start | bytes 6148
  146.1 249.0 %all-reduce.10.cloned.1.call-start = ((), (), s32[]{:S(2)}) async-start(), calls=%async_computation.3 | async-start | bytes 2621440 | tf_op jit(solution)/shard_map/psum | solution.py:40
  155.5 187.2 %copy-start.3 = (bf16[1,384,1280]{2,1,0:T(8,128)(2,1)S(1)}, bf16[1,384,1280]{2,1,0:T(8,128)(2,1)}, u32[]{:S(2)}) copy-start(bf16[1,384,1280]{2,1,0:T(8,128)(2,1)} %param.20) | copy-start | bytes 2949124
  155.5 187.9 %copy-start.11 = (f32[1280]{0:T(1024)S(1)}, f32[1280]{0:T(1024)}, u32[]{:S(2)}) copy-start(f32[1280]{0:T(1024)} %param.32) | copy-start | bytes 15364
  310.9 32.6 %copy-start.5 = (bf16[1280,3,640]{0,2,1:T(8,128)(2,1)S(1)}, bf16[1280,3,640]{0,2,1:T(8,128)(2,1)}, u32[]{:S(2)}) copy-start(bf16[1280,3,640]{0,2,1:T(8,128)(2,1)} %copy.84) | copy-start | bytes 14745604
  359.7 4.6 copy-start.8
  366.6 32.1 %copy-start.12 = (f32[1280]{0:T(1024)S(1)}, f32[1280]{0:T(1024)}, u32[]{:S(2)}) copy-start(f32[1280]{0:T(1024)} %param.33) | copy-start | bytes 15364
  366.6 87.2 %all-reduce.12.cloned.1.call-start = ((), (), s32[]{:S(2)}) async-start(), calls=%async_computation.4 | async-start | bytes 2621440 | tf_op jit(solution)/shard_map/psum | solution.py:47
  398.7 58.5 %copy-start.1 = (bf16[640,1280]{1,0:T(8,128)(2,1)S(1)}, bf16[640,1280]{1,0:T(8,128)(2,1)}, u32[]{:S(2)}) copy-start(bf16[640,1280]{1,0:T(8,128)(2,1)} %param.22) | copy-start | bytes 4915204
Sparse Core Ops, SparseCore 0:
  37.5 35.3 all-reduce.5
  101.3 32.0 all-reduce.7
  146.2 164.6 all-gather.1
  366.7 28.2 all-reduce.9
  421.7 32.0 all-reduce.11
where the time goes:
time: 470 us; the launch traced here: 464 us
  waiting for transfers between devices  283 us (60%)
  matrix products  113 us (24%)
  local copies, waits for them, and re-layouts  31.2 us (7%)
  other arithmetic  19.9 us (4%)
  between operations  13.9 us (3%)
    all_gather x1, waiting for transfers between devices, on_device(): everything = lax.all_gather(merged, 'req', axis=0, tiled=True)  155 us
    psum x2, waiting for transfers between devices, layer(): lax.psum(partial_out.astype(jnp.bfloat16), 'tensor').astype(jnp.float32)  64.4 us
    psum x2, waiting for transfers between devices, layer(): lax.psum(attended.astype(jnp.bfloat16), 'tensor').astype(jnp.float32)  63.4 us
    dot_general x2, matrix products, layer(): partial_out = jnp.dot(hidden, contract, preferred_element_type=jnp.float32)  39.1 us
    dot_general x1, matrix products, on_device(): jnp.einsum('qg,gmc->qmc', matches.astype(jnp.bfloat16), everything, prefe...  29.1 us
    unnamed x32, local copies, waits for them, and re-layouts  17 us
    dot_general x2, matrix products, attend(): jnp.dot(normed, attend_in.reshape(width, -1), preferred_element_type=jnp....  11.3 us
  transfers between devices with their start and end apart: 5, of which 5 were waited for; matrix products, arithmetic and copies ran while one was open for 2% of the time, Pallas kernels for 0%

commit v1 on v0

--- a/solution.py
+++ b/solution.py
@@ -37,7 +37,8 @@
     widened = inputs.astype(jnp.float32)
     first = normalize(widened, gain_first).astype(jnp.bfloat16)
     attended = attend(first, allowed, attend_in, attend_out)
-    residual = widened + lax.psum(attended.astype(jnp.bfloat16), "tensor").astype(jnp.float32)
+    write_hubs = lambda mine: jnp.sum(lax.all_gather(mine, axis_name="tensor"), axis=0)
+    residual = widened + write_hubs(attended.astype(jnp.bfloat16)).astype(jnp.float32)
     second = normalize(residual, gain_second).astype(jnp.bfloat16)
     hidden = jax.nn.gelu(
         jnp.dot(second, expand, preferred_element_type=jnp.float32), approximate=False

time: 470 us -> 442 us (0.940)
  waiting for transfers between devices: 283 us -> 255 us
    psum x2 -> x0, waiting for transfers between devices: 63.4 us -> none  [layer(): lax.psum(attended.astype(jnp.bfloat16), 'tensor').astype(jnp.float32)]
    all_gather x0 -> x2, waiting for transfers between devices: none -> 35 us  [layer(): lax.all_gather(mine, axis_name='tensor')]
    reduce_sum x0 -> x2, other arithmetic: none -> 5.53 us  [layer(): jnp.sum(lax.all_gather(mine, axis_name='tensor'), axis=0)]
where the time goes in v1:
time: 442 us; the launch traced here: 437 us
  waiting for transfers between devices  255 us (58%)
  matrix products  113 us (26%)
  local copies, waits for them, and re-layouts  31.5 us (7%)
  other arithmetic  19.9 us (5%)
  between operations  13.7 us (3%)
    all_gather x1, waiting for transfers between devices, on_device(): everything = lax.all_gather(merged, 'req', axis=0, tiled=True)  156 us
    psum x2, waiting for transfers between devices, layer(): lax.psum(partial_out.astype(jnp.bfloat16), 'tensor').astype(jnp.float32)  64.4 us
    dot_general x2, matrix products, layer(): partial_out = jnp.dot(hidden, contract, preferred_element_type=jnp.float32)  39.1 us
    all_gather x2, waiting for transfers between devices, layer(): lax.all_gather(mine, axis_name='tensor')  35 us
    dot_general x1, matrix products, on_device(): jnp.einsum('qg,gmc->qmc', matches.astype(jnp.bfloat16), everything, prefe...  29.3 us
    unnamed x32, local copies, waits for them, and re-layouts  17.4 us
    dot_general x2, matrix products, attend(): jnp.dot(normed, attend_in.reshape(width, -1), preferred_element_type=jnp....  11.3 us
  transfers between devices with their start and end apart: 5, of which 5 were waited for; matrix products, arithmetic and copies ran while one was open for 2% of the time, Pallas kernels for 0%

profile of v1, /device:TPU:1, one launch (start us, length us, event | category | flops | bytes accessed | tf_op | source)
XLA Modules:
  0.0 436.9 jit_solution(13043119547038196597)
XLA Ops:
  6.5 0.9 constant_dynamic-slice_fusion
  7.4 1.6 convert_reduce_fusion.1
  9.0 1.8 fusion.40
  10.8 8.3 %copy.73 = bf16[1280,3,640]{0,2,1:T(8,128)(2,1)} copy(bf16[1280,3,640]{2,0,1:T(8,128)(2,1)} %param.21) | data formatting | bytes 9830400 | tf_op args[4]
  19.1 6.7 %convolution_convert_fusion.4 = bf16[2,256,1920]{2,1,0:T(8,128)(2,1)} fusion(bf16[1280,1920,1]{0,1,2:T(8,128)(2,1)} %bitcast.115, bf16[2,256,1280]{2,1,0:T(8,128)(2,1)S(1)} %copy-done.2, f32[1280]{0:T(1024)S(1)} %copy-done.9, f32[2,256]{1,0:T(2,128)S(1)} %add_rsqrt_fusion.3, f32[2,256]{1,0:T(2,128)S(1)} %broadcast_multiply_fusion.3), kind=kOutput, calls=%fused_computation.77 | convolution fusion | flops 2520842240 | bytes 8201216 | tf_op jit(solution)/shard_map/dot_general | solution.py:18
  25.8 4.0 copy.75
  29.8 2.0 fusion.147
  31.9 0.1 compare_and_fusion
  31.9 1.5 fusion.223
  33.5 1.6 fusion.116
  35.1 2.3 convolution_convert_fusion.1
  37.4 0.5 all-reduce.4.cloned.1.call-start
  37.9 20.8 %all-gather.8.cloned.1.call-done = bf16[4,256,1280]{2,1,0:T(8,128)(2,1)} async-done(((bf16[2,256,1280]{2,1,0:T(8,128)(2,1)}), bf16[4,256,1280]{2,1,0:T(8,128)(2,1)}) %all-gather.8.cloned.1.call-update) | async-done | bytes 2621456 | tf_op jit(solution)/shard_map/all_gather | solution.py:40
  58.7 2.6 reduce_sum.127
  61.3 0.4 fusion.110
  61.7 0.6 multiply_reduce_fusion.1
  62.4 8.4 %fusion.138 = (u8[256,2560]{1,0:T(8,128)(4,1)S(1)}, u8[256,2560]{1,0:T(8,128)(4,1)S(1)}, f32[2,256,2560]{2,1,0:T(8,128)S(1)}) fusion(bf16[1280,2560]{1,0:T(8,128)(2,1)} %param.23, bf16[2,256,1280]{2,1,0:T(8,128)(2,1)S(1)} %reduce_sum.127, bf16[2,256,1280]{2,1,0:T(8,128)(2,1)S(1)} %copy-done.2, f32[1280]{0:T(1024)S(1)} %copy-done.10, ...), kind=kOutput, calls=%fused_computation.180 | convolution fusion | flops 3375759360 | bytes 15737856 | tf_op jit(solution)/shard_map/dot_general | solution.py:44
  70.8 16.2 %fusion.35 = bf16[2,256,1280]{2,1,0:T(8,128)(2,1)} fusion(bf16[2560,1280]{1,0:T(8,128)(2,1)S(1)} %bitcast.123, f32[2,256,2560]{2,1,0:T(8,128)S(1)} %get-tuple-element.13, u8[256,2560]{1,0:T(8,128)(4,1)S(1)} %get-tuple-element.6, u8[256,2560]{1,0:T(8,128)(4,1)S(1)} %get-tuple-element.5), kind=kOutput, calls=%fused_computation.74 | convolution fusion | flops 3447848960 | bytes 14417920 | tf_op jit(solution)/shard_map/dot_general | solution.py:46
  87.1 32.2 %all-reduce.4.cloned.1.call-done = bf16[2,256,1280]{2,1,0:T(8,128)(2,1)} async-done(((bf16[2,256,1280]{2,1,0:T(8,128)(2,1)}), bf16[2,256,1280]{2,1,0:T(8,128)(2,1)}) %all-reduce.4.cloned.1.call-update) | async-done | bytes 1310736 | tf_op jit(solution)/shard_map/psum | solution.py:48
  119.3 2.8 add_convert_fusion.1
  122.1 3.1 reshape.553
  125.2 1.0 copy.100
  126.2 1.0 reshape.554
  127.2 4.7 %convolution_convert_fusion.5 = bf16[128,640]{1,0:T(8,128)(2,1)} fusion(bf16[128,5120]{1,0:T(8,128)(2,1)S(1)} %reshape.554, bf16[5120,640]{1,0:T(8,128)(2,1)} %param.27), kind=kOutput, calls=%fused_computation.182 | convolution fusion | flops 838942720 | bytes 8028160 | tf_op jit(solution)/shard_map/dot_general | solution.py:97
  132.0 8.4 %copy.84 = bf16[1280,3,640]{0,2,1:T(8,128)(2,1)} copy(bf16[1280,3,640]{2,0,1:T(8,128)(2,1)} %param.28) | data formatting | bytes 9830400 | tf_op args[11]
  140.5 0.1 multiply_reduce_fusion.2
  140.6 0.2 slice_reduce_fusion.1
  140.9 0.1 and.76
  141.0 0.1 fusion.142
  141.2 155.6 %all-gather.6.cloned.1.call-done = bf16[256,64,640]{2,1,0:T(8,128)(2,1)} async-done(((bf16[2,64,640]{2,1,0:T(8,128)(2,1)}), bf16[256,64,640]{2,1,0:T(8,128)(2,1)}) %all-gather.6.cloned.1.call-update) | async-done | bytes 20971536 | tf_op jit(solution)/shard_map/all_gather | solution.py:101
  296.8 29.3 %fusion.139 = bf16[2,64,640]{2,0,1:T(2,128)(2,1)S(1)} fusion(bf16[256,64,640]{2,1,0:T(8,128)(2,1)} %all-gather.6.cloned.1.call-done, s32[256]{0:T(256)S(1)} %copy-done.7, s32[2]{0:T(128)S(1)} %iota_add_fusion), kind=kOutput, calls=%fused_computation.181 | convolution fusion | flops 42025472 | bytes 21136392 | tf_op jit(solution)/shard_map/qg,gmc->qmc/dot_general | solution.py:102
  326.1 2.7 all_gather.21
  328.8 0.2 convert_reduce_fusion
  329.1 0.5 fusion.47
  329.6 4.6 %convolution_convert_fusion.3 = bf16[512,1920]{1,0:T(8,128)(2,1)} fusion(bf16[1280,1920]{0,1:T(8,128)(2,1)S(1)} %bitcast.114, f32[1280]{0:T(1024)S(1)} %copy-done.11, f32[512]{0:T(512)S(1)} %add_rsqrt_fusion.1, f32[512]{0:T(512)S(1)} %broadcast_multiply_fusion.1, bf16[384,1280]{1,0:T(8,128)(2,1)S(1)} %bitcast.104, bf16[128,1280]{1,0:T(8,128)(2,1)S(1)} %all_gather.21), kind=kOutput, calls=%fused_computation.76 | convolution fusion | flops 2522808320 | bytes 8201216 | tf_op jit(solution)/shard_map/dot_general | solution.py:18
  334.2 4.0 copy.85
  338.2 7.7 %fusion.224 = (f32[8,512]{1,0:T(8,128)S(1)}, f32[8,512,512]{1,2,0:T(8,128)}) fusion(pred[512,512]{0,1:T(8,128)(4,1)S(1)} %fusion.142, bf16[1,512,3,8,80]{1,4,3,2,0:T(8,128)(2,1)} %bitcast.118), kind=kOutput, calls=%fused_computation.299 | convolution fusion | flops 343933440 | bytes 9977856 | tf_op jit(solution)/shard_map/sub | solution.py:29
  345.9 4.6 %fusion.117 = bf16[8,80,512]{2,1,0:T(8,128)(2,1)S(1)} fusion(f32[8,512,512]{1,2,0:T(8,128)} %get-tuple-element.15, f32[8,512]{1,0:T(8,128)S(1)} %get-tuple-element.14, bf16[1,512,3,8,80]{1,4,3,2,0:T(8,128)(2,1)} %bitcast.119), kind=kOutput, calls=%fused_computation.161 | convolution fusion | flops 340066304 | bytes 9715712 | tf_op jit(solution)/shard_map/bhqk,bkhd->bqhd/dot_general | solution.py:30
  350.4 2.3 convolution_convert_fusion
  352.7 0.2 all-reduce.6.cloned.1.call-start
  353.0 14.1 %all-gather.10.cloned.1.call-done = bf16[1024,1280]{1,0:T(8,128)(2,1)} async-done(((bf16[512,1280]{1,0:T(8,128)(2,1)}), bf16[1024,1280]{1,0:T(8,128)(2,1)}) %all-gather.10.cloned.1.call-update) | async-done | bytes 2621456 | tf_op jit(solution)/shard_map/all_gather | solution.py:40
  367.1 3.0 reduce.12
  370.1 0.4 fusion.109
  370.5 0.6 copy-done.4
  371.1 0.6 multiply_reduce_fusion
  371.7 22.9 %fusion.38 = bf16[1,512,1280]{2,1,0:T(8,128)(2,1)} fusion(bf16[2560,1280]{1,0:T(8,128)(2,1)} %param.31, bf16[1280,2560]{1,0:T(8,128)(2,1)} %param.30, bf16[512,1280]{1,0:T(8,128)(2,1)} %copy-done.4, f32[1280]{0:T(1024)S(1)} %copy-done.12, f32[512]{0:T(512)S(1)} %add_rsqrt_fusion, f32[512]{0:T(512)S(1)} %broadcast_multiply_fusion, ...), kind=kOutput, calls=%fused_computation.78 | convolution fusion | flops 6803292160 | bytes 17048576 | tf_op jit(solution)/shard_map/dot_general | solution.py:46
  394.6 32.2 %all-reduce.6.cloned.1.call-done = bf16[1,512,1280]{2,1,0:T(8,128)(2,1)} async-done(((bf16[1,512,1280]{2,1,0:T(8,128)(2,1)}), bf16[1,512,1280]{2,1,0:T(8,128)(2,1)}) %all-reduce.6.cloned.1.call-update) | async-done | bytes 1310736 | tf_op jit(solution)/shard_map/psum | solution.py:48
  426.8 3.3 fusion.119
  (54 shorter events, 0.5 us)
Async XLA Ops:
  6.5 28.5 %copy-start = (bf16[640,1280]{1,0:T(8,128)(2,1)S(1)}, bf16[640,1280]{1,0:T(8,128)(2,1)}, u32[]{:S(2)}) copy-start(bf16[640,1280]{1,0:T(8,128)(2,1)} %param.22) | copy-start | bytes 4915204
  6.5 52.2 %all-gather.8.cloned.1.call-start = ((), (), s32[]{:S(2)}) async-start(), calls=%async_computation.3 | async-start | bytes 3932160 | tf_op jit(solution)/shard_map/all_gather | solution.py:40
  10.8 8.3 %copy-start.2 = (bf16[2,256,1280]{2,1,0:T(8,128)(2,1)S(1)}, bf16[2,256,1280]{2,1,0:T(8,128)(2,1)}, u32[]{:S(2)}) copy-start(bf16[2,256,1280]{2,1,0:T(8,128)(2,1)} %param.17) | copy-start | bytes 3932164
  10.8 8.3 %copy-start.9 = (f32[1280]{0:T(1024)S(1)}, f32[1280]{0:T(1024)}, u32[]{:S(2)}) copy-start(f32[1280]{0:T(1024)} %param.25) | copy-start | bytes 15364
  37.4 25.0 %copy-start.10 = (f32[1280]{0:T(1024)S(1)}, f32[1280]{0:T(1024)}, u32[]{:S(2)}) copy-start(f32[1280]{0:T(1024)} %param.26) | copy-start | bytes 15364
  37.4 81.9 %all-reduce.4.cloned.1.call-start = ((), (), s32[]{:S(2)}) async-start(), calls=%async_computation | async-start | bytes 2621440 | tf_op jit(solution)/shard_map/psum | solution.py:48
  61.7 9.1 %slice-start = ((s8[6553600]{0:T(1024)(128)(4,1)}), s8[4194304]{0:T(1024)(128)(4,1)S(1)}, s32[]{:S(2)}) async-start(s8[6553600]{0:T(1024)(128)(4,1)} %bitcast.122), calls=%async_computation.5 | async-start | bytes 8388608
  62.4 8.4 %slice-start.1 = ((s8[6553600]{0:T(1024)(128)(4,1)}), s8[2359296]{0:T(1024)(128)(4,1)S(1)}, s32[]{:S(2)}) async-start(s8[6553600]{0:T(1024)(128)(4,1)} %bitcast.122), calls=%async_computation.6 | async-start | bytes 4718592
  87.0 209.7 %all-gather.6.cloned.1.call-start = ((), (), s32[]{:S(2)}) async-start(), calls=%async_computation.1 | async-start | bytes 21135360 | tf_op jit(solution)/shard_map/all_gather | solution.py:101
  131.9 8.5 %copy-start.7 = (s32[256]{0:T(256)S(1)}, s32[256]{0:T(256)}, u32[]{:S(2)}) copy-start(s32[256]{0:T(256)} %param.19) | copy-start | bytes 3076
  131.9 8.5 %copy-start.6 = (s32[256,2]{0,1:T(2,128)S(1)}, s32[256,2]{0,1:T(2,128)}, u32[]{:S(2)}) copy-start(s32[256,2]{0,1:T(2,128)} %param.18) | copy-start | bytes 6148
  132.0 235.1 %all-gather.10.cloned.1.call-start = ((), (), s32[]{:S(2)}) async-start(), calls=%async_computation.4 | async-start | bytes 3932160 | tf_op jit(solution)/shard_map/all_gather | solution.py:40
  141.1 187.7 %copy-start.3 = (bf16[1,384,1280]{2,1,0:T(8,128)(2,1)S(1)}, bf16[1,384,1280]{2,1,0:T(8,128)(2,1)}, u32[]{:S(2)}) copy-start(bf16[1,384,1280]{2,1,0:T(8,128)(2,1)} %param.20) | copy-start | bytes 2949124
  141.2 188.4 %copy-start.11 = (f32[1280]{0:T(1024)S(1)}, f32[1280]{0:T(1024)}, u32[]{:S(2)}) copy-start(f32[1280]{0:T(1024)} %param.32) | copy-start | bytes 15364
  296.8 32.8 %copy-start.5 = (bf16[1280,3,640]{0,2,1:T(8,128)(2,1)S(1)}, bf16[1280,3,640]{0,2,1:T(8,128)(2,1)}, u32[]{:S(2)}) copy-start(bf16[1280,3,640]{0,2,1:T(8,128)(2,1)} %copy.84) | copy-start | bytes 14745604
  345.9 4.6 %copy-start.8 = (bf16[640,1280]{1,0:T(8,128)(2,1)S(1)}, bf16[640,1280]{1,0:T(8,128)(2,1)}, u32[]{:S(2)}) copy-start(bf16[640,1280]{1,0:T(8,128)(2,1)} %param.29) | copy-start | bytes 4915204
  352.7 19.0 %copy-start.12 = (f32[1280]{0:T(1024)S(1)}, f32[1280]{0:T(1024)}, u32[]{:S(2)}) copy-start(f32[1280]{0:T(1024)} %param.33) | copy-start | bytes 15364
  352.7 74.1 %all-reduce.6.cloned.1.call-start = ((), (), s32[]{:S(2)}) async-start(), calls=%async_computation.2 | async-start | bytes 2621440 | tf_op jit(solution)/shard_map/psum | solution.py:48
  370.1 1.1 copy-start.4
  371.7 58.5 %copy-start.1 = (bf16[640,1280]{1,0:T(8,128)(2,1)S(1)}, bf16[640,1280]{1,0:T(8,128)(2,1)}, u32[]{:S(2)}) copy-start(bf16[640,1280]{1,0:T(8,128)(2,1)} %param.22) | copy-start | bytes 4915204
Sparse Core Ops, SparseCore 0:
  37.5 21.2 all-gather.7
  87.2 32.0 all-reduce.3
  132.1 164.6 all-gather.5
  352.9 14.1 all-gather.9
  394.7 32.0 all-reduce.5
